TPU v7x, 256 devices: a whole 4x4x8 slice. The times are simulated.
256 devices in a mesh: rows: 32 (over y, x, core), cols: 8 (over z).
Axes of the slice: x: 4, y: 4, z: 8, core: 2. Of those that a mesh axis runs over, the one named last changes fastest.
Arguments:
- sheet: bfloat16 [16, 4096, 1024], P('cols', 'rows'), may hold values from -600 to 600
- w_in: bfloat16 [1024, 16, 384], P(None, 'cols'), may hold values from -0.1875 to 0.1875
- w_out: bfloat16 [16, 128, 1024], P('cols'), may hold values from -0.125 to 0.125
Outputs:
- mixed: bfloat16 [16, 4096, 1024], P('cols', 'rows')
All inputs are finite; a program needn't handle non-finite values.
Results may differ from a plain program's by a relative error of at most 0.0067.
Values may be sent and summed in bfloat16 or wider, within the bound.
No kernel may reach another device: no remote copies, remote signals or barrier semaphores. Data moves between devices by JAX's collectives and lax.ppermute only.
A program may use at most 128 MiB of HBM per device.

v0:
```python
import jax
import jax.numpy as jnp
import numpy as np
from jax import lax
from jax.sharding import Mesh, PartitionSpec as P

ROWS_AXES = ("y", "x", "core")


def head_norm(values):
    return values * lax.rsqrt(jnp.mean(values * values, axis=-1, keepdims=True) + 1e-06)


def feature_map(values):
    return jax.nn.elu(values) + 1.0


def finish_proj(proj):
    parts = [
        head_norm(proj[..., 0, :]),
        head_norm(proj[..., 1, :]),
        proj[..., 2, :],
        feature_map(proj[..., 3, :]),
        feature_map(proj[..., 4, :]),
        proj[..., 5, :],
    ]
    return jnp.stack(parts, axis=-2).astype(jnp.bfloat16)


def masked_prefix(gathered, mine):
    idx = lax.broadcasted_iota(jnp.int32, gathered.shape, 0)
    before = jnp.sum(jnp.where(idx < mine, gathered, 0.0), axis=0)
    return (before, jnp.sum(gathered, axis=0))


def exclusive_rows_scan(states):
    core = lax.axis_index("core")
    pair = lax.all_gather(states, "core")
    total = pair[0] + pair[1]
    own = jnp.where(core == 1, pair[0], jnp.zeros_like(pair[0]))
    half = total.shape[0] // 2
    mine = lax.dynamic_slice_in_dim(total, core * half, half, axis=0)
    gx = lax.all_gather(mine, "x")
    xpre, xsum = masked_prefix(gx, lax.axis_index("x"))
    gy = lax.all_gather(xsum, "y")
    ypre, _ = masked_prefix(gy, lax.axis_index("y"))
    chip_prefix = lax.all_gather(ypre + xpre, "core", axis=0, tiled=True)
    return chip_prefix + own


def body(sheet, w_in, w_out):
    high = lax.Precision.HIGHEST
    width = sheet.shape[2]
    heads_here = w_in.shape[1]
    hdim = w_out.shape[1] // 2
    ncols = lax.axis_size("cols")
    core = lax.axis_index("core")
    wh = width // 2
    w_part = lax.dynamic_slice_in_dim(w_out, core * wh, wh, axis=2)
    w_part = lax.all_gather(w_part, "cols", axis=0, tiled=True)
    w_full = lax.all_gather(w_part, "core", axis=2, tiled=True)
    xloc = sheet.astype(jnp.float32)
    normed = (xloc * lax.rsqrt(jnp.mean(xloc * xloc, axis=-1, keepdims=True) + 1e-06)).astype(
        jnp.bfloat16
    )
    piece = lax.all_gather(normed, "cols", axis=0, tiled=True)
    w_flat = w_in.reshape(width, heads_here * 6 * hdim)
    proj = jnp.dot(piece.reshape(-1, width), w_flat, preferred_element_type=jnp.float32)
    all_cols, row_count = (piece.shape[0], piece.shape[1])
    parts = finish_proj(proj.reshape(all_cols, row_count, heads_here, 6, hdim))
    qrow, krow, vrow = (parts[:, :, :, 0], parts[:, :, :, 1], parts[:, :, :, 2])
    fq, fk, vcol = (parts[:, :, :, 3], parts[:, :, :, 4], parts[:, :, :, 5])
    states = jnp.einsum("crhk,crhv->chkv", fk, vcol, preferred_element_type=jnp.float32)
    prior = exclusive_rows_scan(states)
    scale = hdim ** (-0.5)
    score = jnp.einsum("crhd,erhd->rhce", qrow, krow, preferred_element_type=jnp.float32) * scale
    expo = jnp.exp(score)
    weights = (expo / jnp.sum(expo, axis=-1, keepdims=True)).astype(jnp.bfloat16)
    orow = jnp.einsum("rhce,erhd->crhd", weights, vrow, preferred_element_type=jnp.float32).astype(
        jnp.bfloat16
    )
    causal = (jnp.arange(row_count)[:, None] >= jnp.arange(row_count)[None, :]).astype(jnp.float32)
    inner = jnp.einsum("cthd,cshd->chts", fq, fk, preferred_element_type=jnp.float32) * causal
    local = jnp.einsum("chts,cshv->cthv", inner, vcol.astype(jnp.float32), precision=high)
    carried = jnp.einsum("cthk,chkv->cthv", fq.astype(jnp.float32), prior, precision=high)
    ocol = head_norm(carried + local).astype(jnp.bfloat16)
    results = jnp.concatenate([orow, ocol], axis=3)
    mine = lax.all_to_all(results, "cols", 0, 2, tiled=True)
    own_cols = mine.shape[0]
    mixed = jnp.dot(
        mine.reshape(own_cols * row_count, -1),
        w_full.reshape(-1, width),
        preferred_element_type=jnp.float32,
    )
    return mixed.reshape(own_cols, row_count, width).astype(jnp.bfloat16)


def split_mesh(mesh):
    devs = mesh.devices
    n_rows, n_cols = devs.shape
    try:
        nx = len({d.coords[0] for d in devs.flat})
    except Exception:
        nx = 4
    ny = n_rows // (nx * 2)
    return Mesh(devs.reshape(ny, nx, 2, n_cols), ROWS_AXES + ("cols",))


def solution(mesh):
    m4 = split_mesh(mesh)
    spec = P("cols", ROWS_AXES, None)
    return jax.shard_map(
        body,
        mesh=m4,
        in_specs=(spec, P(None, "cols", None), P("cols", None, None)),
        out_specs=spec,
        check_vma=False,
    )
```

profile of v0, /device:TPU:2, one launch (start us, length us, event | category | flops | bytes accessed | tf_op | source)
XLA Modules:
  0.0 267.3 jit_solution(8593396329968372122)
XLA Ops:
  6.5 1.3 fusion.10
  7.8 2.0 fusion.11
  9.8 0.0 all-gather.16.cloned.1.call-start
  9.9 1.7 copy.59
  11.6 1.6 copy.38
  13.3 54.4 %all-gather.10.cloned.1.call-done = bf16[16,128,1024]{2,1,0:T(8,128)(2,1)} async-done(((bf16[2,128,1024]{2,1,0:T(8,128)(2,1)}), bf16[16,128,1024]{2,1,0:T(8,128)(2,1)}) %all-gather.10.cloned.1.call-update) | async-done | bytes 4194320 | tf_op jit(solution)/shard_map/all_gather | solution.py:66
  67.7 5.8 %fusion.43 = (bf16[16,128,2,6,64]{1,4,3,2,0:T(8,128)(2,1)S(1)}, f32[16,128,2,6,64]{1,4,3,2,0:T(8,128)S(1)}) fusion(bf16[2,6,64,1024,1]{3,2,1,0,4:T(8,128)(2,1)} %bitcast.62, bf16[16,128,1024]{2,1,0:T(8,128)(2,1)} %all-gather.10.cloned.1.call-done), kind=kOutput, calls=%fused_computation.67 | convolution fusion | flops 3222798336 | bytes 15204352 | tf_op jit(solution)/shard_map/dot_general | solution.py:68
  73.5 2.6 copy-done.2
  76.2 1.0 copy-done.5
  77.1 1.5 fusion.26
  78.7 0.0 all-gather.20.cloned.1.call-start
  78.7 14.6 %all-gather.16.cloned.1.call-done = f32[32,2,64,64]{3,2,1,0:T(8,128)} async-done(((f32[16,2,64,64]{3,2,1,0:T(8,128)}), f32[32,2,64,64]{3,2,1,0:T(8,128)}) %all-gather.16.cloned.1.call-update) | async-done | bytes 1048592 | tf_op jit(solution)/shard_map/all_gather | solution.py:38
  93.4 1.7 fusion.42
  95.0 0.9 dynamic-slice_add_fusion
  95.9 0.0 all-gather.12.cloned.1.call-start
  96.0 0.8 constant_dynamic-slice_fusion
  96.8 0.0 all-gather.18.cloned.1.call-start
  96.8 32.9 %all-gather.20.cloned.1.call-done = f32[32,2,64,64]{3,2,1,0:T(8,128)} async-done(((f32[8,2,64,64]{3,2,1,0:T(8,128)}), f32[32,2,64,64]{3,2,1,0:T(8,128)}) %all-gather.20.cloned.1.call-update) | async-done | bytes 1048592 | tf_op jit(solution)/shard_map/all_gather | solution.py:43
  129.7 3.1 %select_reduce_fusion = (f32[8,2,64,64]{3,2,1,0:T(8,128)}, f32[8,2,64,64]{3,2,1,0:T(8,128)}) fusion(f32[4,8,2,64,64]{4,3,2,1,0:T(8,128)} %bitcast.59, pred[4]{0:T(512)(128)(4,1)S(1)} %iota_compare_fusion.1), kind=kLoop, calls=%fused_computation.8 | loop fusion | flops 655360 | bytes 1572868 | tf_op jit(solution)/shard_map/reduce_sum | solution.py:32
  132.8 0.2 all-gather.14.cloned.1.call-start
  133.1 40.2 %all-gather.12.cloned.1.call-done = bf16[16,128,512]{2,1,0:T(8,128)(2,1)} async-done(((bf16[2,128,512]{2,1,0:T(8,128)(2,1)}), bf16[16,128,512]{2,1,0:T(8,128)(2,1)}) %all-gather.12.cloned.1.call-update) | async-done | bytes 2097168 | tf_op jit(solution)/shard_map/all_gather | solution.py:60
  173.3 1.9 multiply_reduce_fusion.1
  175.2 1.1 slice_bitcast_fusion.1
  176.3 1.9 fusion.21
  178.2 2.5 copy.43
  180.7 2.5 copy.44
  183.2 2.2 fusion.44
  185.5 1.3 copy.45
  186.8 0.1 fusion.27
  186.9 0.1 divide_convert_fusion
  187.0 1.4 copy.47
  188.4 1.6 copy.46
  190.1 1.7 fusion.45
  191.7 3.0 %copy.48 = bf16[128,2,64,16]{0,2,1,3:T(8,128)(2,1)} copy(bf16[128,2,64,16]{2,3,1,0:T(8,128)(2,1)} %fusion.45) | data formatting | bytes 1048576 | tf_op jit(solution)/shard_map/rhce,erhd->crhd/dot_general | solution.py:79
  194.7 2.6 fusion.37
  197.4 9.5 %all-gather.18.cloned.1.call-done = f32[32,2,64,64]{3,2,1,0:T(8,128)} async-done(((f32[8,2,64,64]{3,2,1,0:T(8,128)}), f32[32,2,64,64]{3,2,1,0:T(8,128)}) %all-gather.18.cloned.1.call-update) | async-done | bytes 1048592 | tf_op jit(solution)/shard_map/all_gather | solution.py:45
  206.9 2.0 select_reduce_fusion.1
  208.8 0.1 add.72
  208.9 2.9 %all_gather.34 = f32[16,2,64,64]{3,2,1,0:T(8,128)S(1)} all-gather(f32[8,2,64,64]{3,2,1,0:T(8,128)S(1)} %add.72), channel_id=1, replica_groups=mesh['y'=4,'x'=4,'core'=2,'cols'=8] {'core'}, dimensions={0}, use_global_device_ids=true | all-gather | bytes 786432 | tf_op jit(solution)/shard_map/all_gather | solution.py:47
  211.8 2.6 fusion.18
  214.4 3.3 %multiply_reduce_fusion = (f32[16,128,2]{1,2,0:T(2,128)S(1)}, f32[16,128,2,64]{1,3,2,0:T(8,128)S(1)}) fusion(f32[16,2,64,128]{3,2,1,0:T(8,128)S(1)} %fusion.18, f32[16,2,128,128]{3,2,1,0:T(8,128)S(1)} %fusion.37, f32[128,128]{1,0:T(8,128)S(1)} %fusion.28, bf16[16,128,2,6,64]{1,4,3,2,0:T(8,128)(2,1)} %copy-done.5), kind=kOutput, calls=%fused_computation.28 | convolution fusion | flops 403959808 | bytes 4800512 | tf_op jit(solution)/shard_map/chts,cshv->cthv/dot_general | solution.py:84
  217.8 0.1 multiply_convert_fusion
  217.9 0.1 pad_maximum_fusion
  218.0 0.8 copy.53
  218.8 35.8 %all_to_all.15 = bf16[16,128,2,128]{3,2,1,0:T(2,128)(2,1)S(1)} all-to-all(bf16[16,128,2,128]{3,2,1,0:T(2,128)(2,1)S(1)} %copy.53), channel_id=1, replica_groups=mesh['y'=4,'x'=4,'core'=2,'cols'=8] {'cols'}, dimensions={0} | all-to-all | bytes 2097152 | tf_op jit(solution)/shard_map/all_to_all | solution.py:88
  254.7 0.7 copy.76
  255.4 0.8 dot_general.39
  256.3 4.2 %convolution_convert_fusion = bf16[2,128,1024]{2,1,0:T(8,128)(2,1)} fusion(bf16[2,128,2048]{2,1,0:T(8,128)(2,1)S(1)} %dot_general.39, bf16[2048,1024,1]{1,0,2:T(8,128)(2,1)} %bitcast.63), kind=kOutput, calls=%fused_computation.14 | convolution fusion | flops 1074003968 | bytes 5767168 | tf_op jit(solution)/shard_map/dot_general | solution.py:90
  (27 shorter events, 0.2 us)
Async XLA Ops:
  6.5 89.4 %copy-start = (bf16[2,128,1024]{2,1,0:T(8,128)(2,1)S(1)}, bf16[2,128,1024]{2,1,0:T(8,128)(2,1)}, u32[]{:S(2)}) copy-start(bf16[2,128,1024]{2,1,0:T(8,128)(2,1)} %param.5) | copy-start | bytes 1572868
  6.5 61.2 %all-gather.10.cloned.1.call-start = ((), (), s32[]{:S(2)}) async-start(), calls=%async_computation.1 | async-start | bytes 4718592 | tf_op jit(solution)/shard_map/all_gather | solution.py:66
  9.8 83.5 %all-gather.16.cloned.1.call-start = ((), (), s32[]{:S(2)}) async-start(), calls=%async_computation.4 | async-start | bytes 3145728 | tf_op jit(solution)/shard_map/all_gather | solution.py:38
  73.5 2.7 copy-start.2
  73.5 3.6 %copy-start.5 = (bf16[16,128,2,6,64]{1,4,3,2,0:T(8,128)(2,1)}, bf16[16,128,2,6,64]{1,4,3,2,0:T(8,128)(2,1)S(1)}, u32[]{:S(2)}) copy-start(bf16[16,128,2,6,64]{1,4,3,2,0:T(8,128)(2,1)S(1)} %get-tuple-element.13) | copy-start | bytes 9437188
  78.7 51.0 %all-gather.20.cloned.1.call-start = ((), (), s32[]{:S(2)}) async-start(), calls=%async_computation.6 | async-start | bytes 2621440 | tf_op jit(solution)/shard_map/all_gather | solution.py:43
  95.9 77.3 %all-gather.12.cloned.1.call-start = ((), (), s32[]{:S(2)}) async-start(), calls=%async_computation.2 | async-start | bytes 2359296 | tf_op jit(solution)/shard_map/all_gather | solution.py:60
  96.8 110.1 %all-gather.18.cloned.1.call-start = ((), (), s32[]{:S(2)}) async-start(), calls=%async_computation.5 | async-start | bytes 2621440 | tf_op jit(solution)/shard_map/all_gather | solution.py:45
  132.8 123.4 %all-gather.14.cloned.1.call-start = ((), (), s32[]{:S(2)}) async-start(), calls=%async_computation.3 | async-start | bytes 6291456 | tf_op jit(solution)/shard_map/all_gather | solution.py:61
  197.4 11.5 %copy-start.3 = (f32[8,2,64,64]{3,2,1,0:T(8,128)S(1)}, f32[8,2,64,64]{3,2,1,0:T(8,128)}, u32[]{:S(2)}) copy-start(f32[8,2,64,64]{3,2,1,0:T(8,128)} %get-tuple-element.7) | copy-start | bytes 786436
  208.8 3.0 %copy-start.1 = (f32[32,2,64,64]{3,2,1,0:T(8,128)S(1)}, f32[32,2,64,64]{3,2,1,0:T(8,128)}, u32[]{:S(2)}) copy-start(f32[32,2,64,64]{3,2,1,0:T(8,128)} %all-gather.16.cloned.1.call-done) | copy-start | bytes 3145732
  214.4 3.5 %copy-start.4 = (bf16[128,2,64,16]{0,2,1,3:T(8,128)(2,1)S(1)}, bf16[128,2,64,16]{0,2,1,3:T(8,128)(2,1)}, u32[]{:S(2)}) copy-start(bf16[128,2,64,16]{0,2,1,3:T(8,128)(2,1)} %copy.48) | copy-start | bytes 1572868
Sparse Core Ops, SparseCore 0:
  10.0 57.6 all-gather.9
  78.8 14.5 all-gather.15
  96.0 33.6 all-gather.19
  131.4 41.8 all-gather.11
  174.9 31.8 all-gather.17
  208.5 19.0 all-gather.13
where the time goes:
time: 268 us; the launch traced here: 267 us
  waiting for transfers between devices  152 us (57%)
  blocking collectives  38.7 us (14%)
  local copies, waits for them, and re-layouts  25.3 us (9%)
  matrix products  24 us (9%)
  between operations  13.8 us (5%)
  other arithmetic  13.4 us (5%)
    all_gather x1, waiting for transfers between devices, body(): piece = lax.all_gather(normed, 'cols', axis=0, tiled=True)  54.4 us
    all_gather x1, waiting for transfers between devices, body(): w_part = lax.all_gather(w_part, 'cols', axis=0, tiled=True)  40.2 us
    all_to_all x1, blocking collectives, body(): mine = lax.all_to_all(results, 'cols', 0, 2, tiled=True)  35.8 us
    all_gather x1, waiting for transfers between devices, exclusive_rows_scan(): gx = lax.all_gather(mine, 'x')  32.9 us
    all_gather x1, waiting for transfers between devices, exclusive_rows_scan(): pair = lax.all_gather(states, 'core')  14.6 us
    all_gather x1, waiting for transfers between devices, exclusive_rows_scan(): gy = lax.all_gather(xsum, 'y')  9.49 us
    squeeze x4, local copies, waits for them, and re-layouts, body(): qrow, krow, vrow = (parts[:, :, :, 0], parts[:, :, :, 1], parts[:, :, :, 2])  7.74 us
    dot_general x1, matrix products, body(): jnp.dot(piece.reshape(-1, width), w_flat, preferred_element_type=jnp.floa...  5.78 us
  transfers between devices with their start and end apart: 6, of which 5 were waited for; matrix products, arithmetic and copies ran while one was open for 16% of the time, Pallas kernels for 0%

commit v1 on v0

--- a/solution.py
+++ b/solution.py
@@ -5,6 +5,13 @@
 from jax.sharding import Mesh, PartitionSpec as P
 
 ROWS_AXES = ("y", "x", "core")
+
+
+def take_the_widths(message, across):
+    return jnp.concatenate(
+        lax.all_to_all(jnp.stack([message for _ in range(lax.axis_size(across))]), across, 0, 0),
+        axis=0,
+    )
 
 
 def head_norm(values):
@@ -57,7 +64,7 @@
     core = lax.axis_index("core")
     wh = width // 2
     w_part = lax.dynamic_slice_in_dim(w_out, core * wh, wh, axis=2)
-    w_part = lax.all_gather(w_part, "cols", axis=0, tiled=True)
+    w_part = take_the_widths(w_part, "cols")
     w_full = lax.all_gather(w_part, "core", axis=2, tiled=True)
     xloc = sheet.astype(jnp.float32)
     normed = (xloc * lax.rsqrt(jnp.mean(xloc * xloc, axis=-1, keepdims=True) + 1e-06)).astype(

time: 268 us -> 228 us (0.85)
  waiting for transfers between devices: 152 us -> 106 us
  starting transfers between devices: 0.39 us -> 4.67 us
    all_gather x1 -> x0, waiting for transfers between devices: 40.2 us -> none  [body(): w_part = lax.all_gather(w_part, 'cols', axis=0, tiled=True)]
    all_gather x1, waiting for transfers between devices: 14.6 us -> 8.76 us  [exclusive_rows_scan(): pair = lax.all_gather(states, 'core')]
    all_to_all x0 -> x1, starting transfers between devices: none -> 4.32 us  [take_the_widths(): lax.all_to_all(jnp.stack([message for _ in range(lax.axis_size(across))])...]
    all_gather x1, waiting for transfers between devices: 9.49 us -> 6.27 us  [exclusive_rows_scan(): gy = lax.all_gather(xsum, 'y')]
    unnamed x13 -> x15, local copies, waits for them, and re-layouts: 5.35 us -> 6.64 us
  transfers between devices with their start and end apart: 6 -> 6, of which waited for: 5 -> 5; matrix products, arithmetic and copies ran while one was open for 16% -> 20% of each run, Pallas kernels for 0% -> 0%
where the time goes in v1:
time: 228 us
  waiting for transfers between devices  106 us (46%)
  blocking collectives  38.7 us (17%)
  local copies, waits for them, and re-layouts  27.4 us (12%)
  matrix products  24.1 us (11%)
  other arithmetic  13.4 us (6%)
  between operations  13.4 us (6%)
  starting transfers between devices  4.67 us (2%)
    all_gather x1, waiting for transfers between devices, body(): piece = lax.all_gather(normed, 'cols', axis=0, tiled=True)  54.4 us
    all_to_all x1, blocking collectives, body(): mine = lax.all_to_all(results, 'cols', 0, 2, tiled=True)  35.8 us
    all_gather x1, waiting for transfers between devices, exclusive_rows_scan(): gx = lax.all_gather(mine, 'x')  33.7 us
    all_gather x1, waiting for transfers between devices, exclusive_rows_scan(): pair = lax.all_gather(states, 'core')  8.76 us
    squeeze x4, local copies, waits for them, and re-layouts, body(): qrow, krow, vrow = (parts[:, :, :, 0], parts[:, :, :, 1], parts[:, :, :, 2])  7.74 us
    unnamed x15, local copies, waits for them, and re-layouts  6.64 us
    all_gather x1, waiting for transfers between devices, exclusive_rows_scan(): gy = lax.all_gather(xsum, 'y')  6.27 us
    dot_general x1, matrix products, body(): jnp.dot(piece.reshape(-1, width), w_flat, preferred_element_type=jnp.floa...  5.78 us
  transfers between devices with their start and end apart: 6, of which 5 were waited for; matrix products, arithmetic and copies ran while one was open for 20% of the time, Pallas kernels for 0%

profile of v1, /device:TPU:2, one launch (start us, length us, event | category | flops | bytes accessed | tf_op | source)
XLA Modules:
  0.0 227.5 jit_solution(1230211027453386069)
XLA Ops:
  6.5 1.3 fusion.10
  7.8 2.0 fusion.11
  9.8 0.0 all-gather.13.cloned.1.call-start
  9.9 1.7 copy.59
  11.6 1.6 copy.38
  13.3 54.4 %all-gather.9.cloned.1.call-done = bf16[16,128,1024]{2,1,0:T(8,128)(2,1)} async-done(((bf16[2,128,1024]{2,1,0:T(8,128)(2,1)}), bf16[16,128,1024]{2,1,0:T(8,128)(2,1)}) %all-gather.9.cloned.1.call-update) | async-done | bytes 4194320 | tf_op jit(solution)/shard_map/all_gather | solution.py:73
  67.7 5.8 %fusion.43 = (bf16[16,128,2,6,64]{1,4,3,2,0:T(8,128)(2,1)S(1)}, f32[16,128,2,6,64]{1,4,3,2,0:T(8,128)S(1)}) fusion(bf16[2,6,64,1024,1]{3,2,1,0,4:T(8,128)(2,1)} %bitcast.64, bf16[16,128,1024]{2,1,0:T(8,128)(2,1)} %all-gather.9.cloned.1.call-done), kind=kOutput, calls=%fused_computation.67 | convolution fusion | flops 3222798336 | bytes 15204352 | tf_op jit(solution)/shard_map/dot_general | solution.py:75
  73.5 2.6 %copy-done.3 = f32[16,128,2,6,64]{1,4,3,2,0:T(8,128)} copy-done((f32[16,128,2,6,64]{1,4,3,2,0:T(8,128)}, f32[16,128,2,6,64]{1,4,3,2,0:T(8,128)S(1)}, u32[]{:S(2)}) %copy-start.3) | copy-done | bytes 6291480
  76.2 1.0 copy-done.6
  77.1 1.5 fusion.26
  78.7 1.5 stack.3
  80.2 4.3 %all-to-all-start.1 = ((bf16[8,2,128,512]{3,2,1,0:T(8,128)(2,1)}), bf16[8,2,128,512]{3,2,1,0:T(8,128)(2,1)S(1)}, u32[]{:S(2)}, u32[]{:S(2)}) async-start(bf16[8,2,128,512]{3,2,1,0:T(8,128)(2,1)} %stack.3), calls=%async_computation.1 | async-start | bytes 4194304 | tf_op jit(solution)/shard_map/all_to_all | solution.py:12
  84.6 8.8 %all-gather.13.cloned.1.call-done = f32[32,2,64,64]{3,2,1,0:T(8,128)} async-done(((f32[16,2,64,64]{3,2,1,0:T(8,128)}), f32[32,2,64,64]{3,2,1,0:T(8,128)}) %all-gather.13.cloned.1.call-update) | async-done | bytes 1048592 | tf_op jit(solution)/shard_map/all_gather | solution.py:45
  93.4 1.7 fusion.42
  95.0 0.9 dynamic-slice_add_fusion
  95.9 0.0 all-gather.15.cloned.1.call-start
  96.0 33.7 %all-gather.17.cloned.1.call-done = f32[32,2,64,64]{3,2,1,0:T(8,128)} async-done(((f32[8,2,64,64]{3,2,1,0:T(8,128)}), f32[32,2,64,64]{3,2,1,0:T(8,128)}) %all-gather.17.cloned.1.call-update) | async-done | bytes 1048592 | tf_op jit(solution)/shard_map/all_gather | solution.py:50
  129.7 3.1 %select_reduce_fusion = (f32[8,2,64,64]{3,2,1,0:T(8,128)}, f32[8,2,64,64]{3,2,1,0:T(8,128)}) fusion(f32[4,8,2,64,64]{4,3,2,1,0:T(8,128)} %bitcast.61, pred[4]{0:T(512)(128)(4,1)S(1)} %iota_compare_fusion.1), kind=kLoop, calls=%fused_computation.8 | loop fusion | flops 655360 | bytes 1572868 | tf_op jit(solution)/shard_map/reduce_sum | solution.py:39
  132.8 0.2 all-gather.11.cloned.1.call-start
  133.1 2.5 %all-to-all-done.1 = bf16[8,2,128,512]{3,2,1,0:T(8,128)(2,1)S(1)} async-done(((bf16[8,2,128,512]{3,2,1,0:T(8,128)(2,1)}), bf16[8,2,128,512]{3,2,1,0:T(8,128)(2,1)S(1)}, u32[]{:S(2)}, u32[]{:S(2)}) %all-to-all-start.1) | async-done | bytes 2097184 | tf_op jit(solution)/shard_map/all_to_all | solution.py:12
  135.6 1.3 copy-done.1
  136.9 1.9 multiply_reduce_fusion.1
  138.8 1.1 slice_bitcast_fusion.1
  140.0 1.9 fusion.21
  141.8 2.5 %copy.43 = bf16[16,128,2,64]{3,0,2,1:T(8,128)(2,1)} copy(bf16[16,128,2,64]{1,3,2,0:T(8,128)(2,1)S(1)} %get-tuple-element.10) | data formatting | bytes 1048576 | tf_op jit(solution)/shard_map/squeeze | solution.py:78
  144.4 2.5 %copy.44 = bf16[16,128,2,64]{3,0,2,1:T(8,128)(2,1)} copy(bf16[16,128,2,64]{1,3,2,0:T(8,128)(2,1)S(1)} %get-tuple-element.9) | data formatting | bytes 1048576 | tf_op jit(solution)/shard_map/squeeze | solution.py:78
  146.9 2.3 %fusion.44 = f32[128,2,16,16]{2,3,1,0:T(8,128)S(1)} fusion(bf16[16,128,2,64]{3,0,2,1:T(8,128)(2,1)} %copy.43, bf16[16,128,2,64]{3,0,2,1:T(8,128)(2,1)} %copy.44), kind=kOutput, calls=%fused_computation.68 | convolution fusion | flops 8388608 | bytes 1310720 | tf_op jit(solution)/shard_map/crhd,erhd->rhce/dot_general | solution.py:83
  149.2 1.3 copy.45
  150.6 0.1 fusion.27
  150.6 0.1 divide_convert_fusion
  150.7 1.4 copy.47
  152.2 1.6 copy.46
  153.8 1.7 fusion.45
  155.4 3.0 %copy.48 = bf16[128,2,64,16]{0,2,1,3:T(8,128)(2,1)} copy(bf16[128,2,64,16]{2,3,1,0:T(8,128)(2,1)} %fusion.45) | data formatting | bytes 1048576 | tf_op jit(solution)/shard_map/rhce,erhd->crhd/dot_general | solution.py:86
  158.4 2.6 %fusion.37 = f32[16,2,128,128]{3,2,1,0:T(8,128)S(1)} fusion(f32[16,128,2,6,64]{1,4,3,2,0:T(8,128)} %copy-done.3), kind=kOutput, calls=%fused_computation.65 | convolution fusion | flops 69730304 | bytes 4194304 | tf_op jit(solution)/shard_map/cthd,cshd->chts/dot_general | solution.py:90
  161.1 6.3 %all-gather.15.cloned.1.call-done = f32[32,2,64,64]{3,2,1,0:T(8,128)} async-done(((f32[8,2,64,64]{3,2,1,0:T(8,128)}), f32[32,2,64,64]{3,2,1,0:T(8,128)}) %all-gather.15.cloned.1.call-update) | async-done | bytes 1048592 | tf_op jit(solution)/shard_map/all_gather | solution.py:52
  167.3 2.0 select_reduce_fusion.1
  169.3 0.1 add.72
  169.4 2.9 %all_gather.31 = f32[16,2,64,64]{3,2,1,0:T(8,128)S(1)} all-gather(f32[8,2,64,64]{3,2,1,0:T(8,128)S(1)} %add.72), channel_id=1, replica_groups=mesh['y'=4,'x'=4,'core'=2,'cols'=8] {'core'}, dimensions={0}, use_global_device_ids=true | all-gather | bytes 786432 | tf_op jit(solution)/shard_map/all_gather | solution.py:54
  172.3 2.6 %fusion.18 = f32[16,2,64,128]{3,2,1,0:T(8,128)S(1)} fusion(f32[16,2,64,64]{3,2,1,0:T(8,128)S(1)} %all_gather.31, pred[]{:T(512)S(6)} %eq.3, f32[32,2,64,64]{3,2,1,0:T(8,128)S(1)} %copy-done.2, f32[16,128,2,6,64]{1,4,3,2,0:T(8,128)} %copy-done.3), kind=kOutput, calls=%fused_computation.26 | convolution fusion | flops 202899456 | bytes 4194305 | tf_op jit(solution)/shard_map/cthk,chkv->cthv/dot_general | solution.py:92
  174.9 3.3 %multiply_reduce_fusion = (f32[16,128,2]{1,2,0:T(2,128)S(1)}, f32[16,128,2,64]{1,3,2,0:T(8,128)S(1)}) fusion(f32[16,2,64,128]{3,2,1,0:T(8,128)S(1)} %fusion.18, f32[16,2,128,128]{3,2,1,0:T(8,128)S(1)} %fusion.37, f32[128,128]{1,0:T(8,128)S(1)} %fusion.28, bf16[16,128,2,6,64]{1,4,3,2,0:T(8,128)(2,1)} %copy-done.6), kind=kOutput, calls=%fused_computation.28 | convolution fusion | flops 403959808 | bytes 4800512 | tf_op jit(solution)/shard_map/chts,cshv->cthv/dot_general | solution.py:91
  178.3 0.1 multiply_convert_fusion
  178.4 0.1 pad_maximum_fusion
  178.5 0.8 copy.53
  179.3 35.8 %all_to_all.20 = bf16[16,128,2,128]{3,2,1,0:T(2,128)(2,1)S(1)} all-to-all(bf16[16,128,2,128]{3,2,1,0:T(2,128)(2,1)S(1)} %copy.53), channel_id=1, replica_groups=mesh['y'=4,'x'=4,'core'=2,'cols'=8] {'cols'}, dimensions={0} | all-to-all | bytes 2097152 | tf_op jit(solution)/shard_map/all_to_all | solution.py:95
  215.2 0.7 copy.76
  215.9 0.8 dot_general.39
  216.8 4.2 %convolution_convert_fusion = bf16[2,128,1024]{2,1,0:T(8,128)(2,1)} fusion(bf16[2,128,2048]{2,1,0:T(8,128)(2,1)S(1)} %dot_general.39, bf16[2048,1024,1]{1,0,2:T(8,128)(2,1)} %bitcast.65), kind=kOutput, calls=%fused_computation.14 | convolution fusion | flops 1074003968 | bytes 5767168 | tf_op jit(solution)/shard_map/dot_general | solution.py:97
  (29 shorter events, 0.3 us)
Async XLA Ops:
  6.5 72.2 %copy-start = (bf16[2,128,1024]{2,1,0:T(8,128)(2,1)S(1)}, bf16[2,128,1024]{2,1,0:T(8,128)(2,1)}, u32[]{:S(2)}) copy-start(bf16[2,128,1024]{2,1,0:T(8,128)(2,1)} %param.5) | copy-start | bytes 1572868
  6.5 61.2 %all-gather.9.cloned.1.call-start = ((), (), s32[]{:S(2)}) async-start(), calls=%async_computation.2 | async-start | bytes 4718592 | tf_op jit(solution)/shard_map/all_gather | solution.py:73
  9.8 83.5 %all-gather.13.cloned.1.call-start = ((), (), s32[]{:S(2)}) async-start(), calls=%async_computation.4 | async-start | bytes 3145728 | tf_op jit(solution)/shard_map/all_gather | solution.py:45
  73.5 2.7 %copy-start.3 = (f32[16,128,2,6,64]{1,4,3,2,0:T(8,128)}, f32[16,128,2,6,64]{1,4,3,2,0:T(8,128)S(1)}, u32[]{:S(2)}) copy-start(f32[16,128,2,6,64]{1,4,3,2,0:T(8,128)S(1)} %get-tuple-element.14) | copy-start | bytes 18874372
  73.5 3.6 %copy-start.6 = (bf16[16,128,2,6,64]{1,4,3,2,0:T(8,128)(2,1)}, bf16[16,128,2,6,64]{1,4,3,2,0:T(8,128)(2,1)S(1)}, u32[]{:S(2)}) copy-start(bf16[16,128,2,6,64]{1,4,3,2,0:T(8,128)(2,1)S(1)} %get-tuple-element.13) | copy-start | bytes 9437188
  80.2 55.4 %all-to-all-start.1 = ((bf16[8,2,128,512]{3,2,1,0:T(8,128)(2,1)}), bf16[8,2,128,512]{3,2,1,0:T(8,128)(2,1)S(1)}, u32[]{:S(2)}, u32[]{:S(2)}) async-start(bf16[8,2,128,512]{3,2,1,0:T(8,128)(2,1)} %stack.3), calls=%async_computation.1 | async-start | bytes 4194304 | tf_op jit(solution)/shard_map/all_to_all | solution.py:12
  84.6 45.2 %all-gather.17.cloned.1.call-start = ((), (), s32[]{:S(2)}) async-start(), calls=%async_computation.6 | async-start | bytes 2621440 | tf_op jit(solution)/shard_map/all_gather | solution.py:50
  95.9 71.4 %all-gather.15.cloned.1.call-start = ((), (), s32[]{:S(2)}) async-start(), calls=%async_computation.5 | async-start | bytes 2621440 | tf_op jit(solution)/shard_map/all_gather | solution.py:52
  132.8 83.9 %all-gather.11.cloned.1.call-start = ((), (), s32[]{:S(2)}) async-start(), calls=%async_computation.3 | async-start | bytes 6291456 | tf_op jit(solution)/shard_map/all_gather | solution.py:68
  135.6 1.3 copy-start.1
  161.1 8.3 %copy-start.4 = (f32[8,2,64,64]{3,2,1,0:T(8,128)S(1)}, f32[8,2,64,64]{3,2,1,0:T(8,128)}, u32[]{:S(2)}) copy-start(f32[8,2,64,64]{3,2,1,0:T(8,128)} %get-tuple-element.7) | copy-start | bytes 786436
  169.3 3.0 %copy-start.2 = (f32[32,2,64,64]{3,2,1,0:T(8,128)S(1)}, f32[32,2,64,64]{3,2,1,0:T(8,128)}, u32[]{:S(2)}) copy-start(f32[32,2,64,64]{3,2,1,0:T(8,128)} %all-gather.13.cloned.1.call-done) | copy-start | bytes 3145732
  174.9 3.5 %copy-start.5 = (bf16[128,2,64,16]{0,2,1,3:T(8,128)(2,1)S(1)}, bf16[128,2,64,16]{0,2,1,3:T(8,128)(2,1)}, u32[]{:S(2)}) copy-start(bf16[128,2,64,16]{0,2,1,3:T(8,128)(2,1)} %copy.48) | copy-start | bytes 1572868
Sparse Core Ops, SparseCore 0:
  10.0 57.6 all-gather.8
  78.8 14.5 all-gather.12
  96.0 33.6 all-gather.16
  133.0 34.3 all-gather.14
  169.0 19.0 all-gather.10
